TPU v7x, 512 devices: a whole 4x8x8 slice. The times are simulated.
512 devices in a mesh: param: 32 (over x, z), ex: 16 (over y, core).
Axes of the slice: x: 4, y: 8, z: 8, core: 2. Of those that a mesh axis runs over, the one named last changes fastest.
Arguments:
- adapter_gradients: bfloat16 [512, 131072], P('ex', 'param'), may hold values from -560 to 560
- sign_hash_keys: int32 [4], replicated, may hold values from 1 to 16777215
- target_indices: int32 [256], replicated, may hold values from 0 to 511
Outputs:
- features: float32 [512, 8192], P('ex', 'param')
- scores: float32 [512, 256], P('ex')
All inputs are finite; a program needn't handle non-finite values.
Results may differ from a plain program's by a relative error of at most 0.0003.
Values sent between devices are 32-bit elements; how exact they have to be, the bound alone decides.
No kernel may reach another device: no remote copies, remote signals or barrier semaphores. Data moves between devices by JAX's collectives and lax.ppermute only.
A program may use at most 128 MiB of HBM per device.

v0:
```python
import jax
import jax.numpy as jnp
from jax import lax
from jax.sharding import PartitionSpec as P

K = 8192
norm_eps = 1e-06


def sign_block(sign_hash_keys, first_row, row_count, col_count):
    mult_row = sign_hash_keys[0] | 1
    mult_col = sign_hash_keys[1] | 1
    seed_add = sign_hash_keys[2]
    mix_mult = sign_hash_keys[3] | 1
    row_ids = first_row + lax.iota(jnp.int32, row_count)[:, None]
    col_ids = lax.iota(jnp.int32, col_count)[None, :]
    hashed = row_ids * mult_row + col_ids * mult_col + seed_add
    hashed = hashed ^ lax.shift_right_logical(hashed, jnp.full_like(hashed, 16))
    hashed = hashed * mix_mult
    hashed = hashed ^ lax.shift_right_logical(hashed, jnp.full_like(hashed, 13))
    hashed = hashed * jnp.int32(-1028477387)
    hashed = hashed ^ lax.shift_right_logical(hashed, jnp.full_like(hashed, 16))
    return jnp.where(hashed < 0, 1.0, -1.0).astype(jnp.bfloat16)


def local(adapter_gradients, sign_hash_keys, target_indices):
    resident_example, resident_rows = adapter_gradients.shape
    row_base = lax.axis_index("param") * jnp.int32(resident_rows)
    turn_count = 8
    rows_per_tile = resident_rows // turn_count
    scale_k = jnp.float32(K)

    def accumulate(tile_idx, totals):
        start_offset = tile_idx * jnp.int32(rows_per_tile)
        gradient_slab = lax.dynamic_slice_in_dim(adapter_gradients, start_offset, rows_per_tile, 1)
        signs = sign_block(sign_hash_keys, row_base + start_offset, rows_per_tile, K)
        return totals + jnp.dot(gradient_slab, signs, preferred_element_type=jnp.float32)

    partial_sums = lax.fori_loop(
        jnp.int32(0),
        jnp.int32(turn_count),
        accumulate,
        jnp.zeros((resident_example, K), jnp.float32),
    )
    projected = lax.psum_scatter(partial_sums, "param", scatter_dimension=1, tiled=True)
    own_squares = jnp.sum(projected * projected, axis=1)
    total_sq = lax.psum(own_squares, "param")
    features = projected * jnp.sqrt(scale_k / (total_sq + norm_eps))[:, None]
    pool_rows = lax.all_gather(features, "ex", axis=0, tiled=True)
    targets = jnp.take(pool_rows, target_indices, axis=0)
    partial_dots = jnp.dot(features, targets.T, precision=lax.Precision.HIGHEST)
    scores = lax.psum(partial_dots, "param") / scale_k
    return (features, scores)


def solution(mesh):
    return jax.shard_map(
        local,
        mesh=mesh,
        in_specs=(P("ex", "param"), P(), P()),
        out_specs=(P("ex", "param"), P("ex", None)),
        check_vma=False,
    )
```

profile of v0, /device:TPU:8, one launch (start us, length us, event | category | flops | bytes accessed | tf_op | source)
XLA Modules:
  0.0 555.2 jit_solution(16775991105922428957)
XLA Ops:
  7.2 0.0 reduce-scatter.2.cloned.1.call-start
  7.2 1.4 fusion.24
  10.4 81.0 %while.12 = (s32[]{:T(128)}, f32[32,8192]{1,0:T(8,128)S(1)}, bf16[32,4096]{1,0:T(8,128)(2,1)}, s32[]{:T(128)}, s32[]{:T(128)}, /*index=5*/s32[]{:T(128)}, s32[4]...) while((s32[]{:T(128)}, f32[32,8192]{1,0:T(8,128)S(1)}, ...), condition=%wide.region_1.2_spmd.clone, body=%wide.region_0.1_spmd.clone.sunk | while | flops 323494912 | bytes 2200785 | solution.py:39
  10.5 1.3 slice.29
  11.8 8.8 %convolution_add_fusion.2 = f32[32,8192]{1,0:T(8,128)S(1)} fusion(s32[]{:T(128)} %get-tuple-element.187, s32[]{:T(128)} %bitcast.6, s32[8192]{0:T(1024)S(1)} %iota_multiply_fusion.2, s32[512]{0:T(512)S(1)} %add_multiply_fusion.2, f32[32,8192]{1,0:T(8,128)S(1)} %get-tuple-element.169, pred[]{:T(512)S(6)} %compare.3, ...), kind=kOutput, calls=%fused_computation.8.clone.1 | convolution fusion | flops 323485696 | bytes 2165765 | tf_op jit(solution)/shard_map/while/body/dot_general | solution.py:37
  20.6 1.3 slice.29
  21.9 8.8 %convolution_add_fusion.2 = f32[32,8192]{1,0:T(8,128)S(1)} fusion(s32[]{:T(128)} %get-tuple-element.187, s32[]{:T(128)} %bitcast.6, s32[8192]{0:T(1024)S(1)} %iota_multiply_fusion.2, s32[512]{0:T(512)S(1)} %add_multiply_fusion.2, f32[32,8192]{1,0:T(8,128)S(1)} %get-tuple-element.169, pred[]{:T(512)S(6)} %compare.3, ...), kind=kOutput, calls=%fused_computation.8.clone.1 | convolution fusion | flops 323485696 | bytes 2165765 | tf_op jit(solution)/shard_map/while/body/dot_general | solution.py:37
  30.8 1.3 slice.29
  32.1 8.8 %convolution_add_fusion.2 = f32[32,8192]{1,0:T(8,128)S(1)} fusion(s32[]{:T(128)} %get-tuple-element.187, s32[]{:T(128)} %bitcast.6, s32[8192]{0:T(1024)S(1)} %iota_multiply_fusion.2, s32[512]{0:T(512)S(1)} %add_multiply_fusion.2, f32[32,8192]{1,0:T(8,128)S(1)} %get-tuple-element.169, pred[]{:T(512)S(6)} %compare.3, ...), kind=kOutput, calls=%fused_computation.8.clone.1 | convolution fusion | flops 323485696 | bytes 2165765 | tf_op jit(solution)/shard_map/while/body/dot_general | solution.py:37
  40.9 1.3 slice.29
  42.2 8.8 %convolution_add_fusion.2 = f32[32,8192]{1,0:T(8,128)S(1)} fusion(s32[]{:T(128)} %get-tuple-element.187, s32[]{:T(128)} %bitcast.6, s32[8192]{0:T(1024)S(1)} %iota_multiply_fusion.2, s32[512]{0:T(512)S(1)} %add_multiply_fusion.2, f32[32,8192]{1,0:T(8,128)S(1)} %get-tuple-element.169, pred[]{:T(512)S(6)} %compare.3, ...), kind=kOutput, calls=%fused_computation.8.clone.1 | convolution fusion | flops 323485696 | bytes 2165765 | tf_op jit(solution)/shard_map/while/body/dot_general | solution.py:37
  51.0 1.3 slice.29
  52.3 8.8 %convolution_add_fusion.2 = f32[32,8192]{1,0:T(8,128)S(1)} fusion(s32[]{:T(128)} %get-tuple-element.187, s32[]{:T(128)} %bitcast.6, s32[8192]{0:T(1024)S(1)} %iota_multiply_fusion.2, s32[512]{0:T(512)S(1)} %add_multiply_fusion.2, f32[32,8192]{1,0:T(8,128)S(1)} %get-tuple-element.169, pred[]{:T(512)S(6)} %compare.3, ...), kind=kOutput, calls=%fused_computation.8.clone.1 | convolution fusion | flops 323485696 | bytes 2165765 | tf_op jit(solution)/shard_map/while/body/dot_general | solution.py:37
  61.1 1.3 slice.29
  62.4 8.8 %convolution_add_fusion.2 = f32[32,8192]{1,0:T(8,128)S(1)} fusion(s32[]{:T(128)} %get-tuple-element.187, s32[]{:T(128)} %bitcast.6, s32[8192]{0:T(1024)S(1)} %iota_multiply_fusion.2, s32[512]{0:T(512)S(1)} %add_multiply_fusion.2, f32[32,8192]{1,0:T(8,128)S(1)} %get-tuple-element.169, pred[]{:T(512)S(6)} %compare.3, ...), kind=kOutput, calls=%fused_computation.8.clone.1 | convolution fusion | flops 323485696 | bytes 2165765 | tf_op jit(solution)/shard_map/while/body/dot_general | solution.py:37
  71.3 1.3 slice.29
  72.6 8.8 %convolution_add_fusion.2 = f32[32,8192]{1,0:T(8,128)S(1)} fusion(s32[]{:T(128)} %get-tuple-element.187, s32[]{:T(128)} %bitcast.6, s32[8192]{0:T(1024)S(1)} %iota_multiply_fusion.2, s32[512]{0:T(512)S(1)} %add_multiply_fusion.2, f32[32,8192]{1,0:T(8,128)S(1)} %get-tuple-element.169, pred[]{:T(512)S(6)} %compare.3, ...), kind=kOutput, calls=%fused_computation.8.clone.1 | convolution fusion | flops 323485696 | bytes 2165765 | tf_op jit(solution)/shard_map/while/body/dot_general | solution.py:37
  81.4 1.3 slice.29
  82.7 8.8 %convolution_add_fusion.2 = f32[32,8192]{1,0:T(8,128)S(1)} fusion(s32[]{:T(128)} %get-tuple-element.187, s32[]{:T(128)} %bitcast.6, s32[8192]{0:T(1024)S(1)} %iota_multiply_fusion.2, s32[512]{0:T(512)S(1)} %add_multiply_fusion.2, f32[32,8192]{1,0:T(8,128)S(1)} %get-tuple-element.169, pred[]{:T(512)S(6)} %compare.3, ...), kind=kOutput, calls=%fused_computation.8.clone.1 | convolution fusion | flops 323485696 | bytes 2165765 | tf_op jit(solution)/shard_map/while/body/dot_general | solution.py:37
  91.5 0.0 copy-start.2
  91.5 1.0 copy-done
  92.5 0.0 reduce-scatter.2.cloned.1.call-update
  92.5 225.0 %reduce-scatter.2.cloned.1.call-done = f32[32,256]{1,0:T(8,128)} async-done(((f32[32,8192]{1,0:T(8,128)}), f32[32,256]{1,0:T(8,128)}) %reduce-scatter.2.cloned.1.call-update) | async-done | bytes 32784 | tf_op jit(solution)/shard_map/reduce_scatter | solution.py:45
  317.6 0.9 multiply_reduce_fusion
  318.4 72.3 %psum.14 = f32[32]{0:T(128)S(1)} all-reduce(f32[32]{0:T(128)S(1)} %multiply_reduce_fusion), channel_id=1, replica_groups=mesh['param'=32,'ex'=16] {'param'}, use_global_device_ids=true, to_apply=%region_4.5 | all-reduce | flops 32 | bytes 256 | tf_op jit(solution)/shard_map/psum | solution.py:47
  390.7 0.8 broadcast_multiply_fusion.1
  391.5 17.1 %all_gather.3 = f32[512,256]{1,0:T(8,128)S(1)} all-gather(f32[32,256]{1,0:T(8,128)S(1)} %broadcast_multiply_fusion.1), channel_id=1, replica_groups=mesh['param'=32,'ex'=16] {'ex'}, dimensions={0}, use_global_device_ids=true | all-gather | bytes 557056 | tf_op jit(solution)/shard_map/all_gather | solution.py:49
  408.7 1.0 gather_fusion
  409.6 0.0 copy-done.1
  409.6 0.4 fusion.19
  410.1 137.7 %psum.15 = f32[32,256]{1,0:T(8,128)S(1)} all-reduce(f32[32,256]{1,0:T(8,128)S(1)} %fusion.19), channel_id=1, replica_groups=mesh['param'=32,'ex'=16] {'param'}, use_global_device_ids=true, to_apply=%region_5.6 | all-reduce | flops 8192 | bytes 65536 | tf_op jit(solution)/shard_map/psum | solution.py:52
  547.7 0.6 broadcast_multiply_fusion
  (24 shorter events, 0.2 us)
Async XLA Ops:
  7.2 310.4 %reduce-scatter.2.cloned.1.call-start = ((), (), s32[]{:S(2)}) async-start(), calls=%async_computation.1 | async-start | bytes 1081344 | tf_op jit(solution)/shard_map/reduce_scatter | solution.py:45
  91.5 1.0 copy-start
  91.5 1.0 copy-start.2
  391.5 18.1 %copy-start.1 = (f32[32,256]{1,0:T(8,128)}, f32[32,256]{1,0:T(8,128)S(1)}, u32[]{:S(2)}) copy-start(f32[32,256]{1,0:T(8,128)S(1)} %broadcast_multiply_fusion.1) | copy-start | bytes 98308
Sparse Core Ops, SparseCore 0:
  92.6 224.9 reduce-scatter.1
where the time goes:
time: 556 us; the launch traced here: 555 us
  blocking collectives  227 us (41%)
  waiting for transfers between devices  225 us (40%)
  matrix products  70.5 us (13%)
  between operations  16 us (3%)
  local copies, waits for them, and re-layouts  13.7 us (2%)
    reduce_scatter x1, waiting for transfers between devices, local(): lax.psum_scatter(partial_sums, 'param', scatter_dimension=1, tiled=True)  225 us
    psum x1, blocking collectives, local(): scores = lax.psum(partial_dots, 'param') / scale_k  138 us
    psum x1, blocking collectives, local(): total_sq = lax.psum(own_squares, 'param')  72.3 us
    dot_general x8, matrix products, accumulate(): jnp.dot(gradient_slab, signs, preferred_element_type=jnp.float32)  70 us
    all_gather x1, blocking collectives, local(): pool_rows = lax.all_gather(features, 'ex', axis=0, tiled=True)  17.1 us
  transfers between devices with their start and end apart: 1, of which 1 were waited for; matrix products, arithmetic and copies ran while one was open for 0% of the time, Pallas kernels for 0%

commit v1 on v0

--- a/solution.py
+++ b/solution.py
@@ -46,7 +46,24 @@
     own_squares = jnp.sum(projected * projected, axis=1)
     total_sq = lax.psum(own_squares, "param")
     features = projected * jnp.sqrt(scale_k / (total_sq + norm_eps))[:, None]
-    pool_rows = lax.all_gather(features, "ex", axis=0, tiled=True)
+    peers, index, width = (lax.axis_size("ex"), lax.axis_index("ex"), features.shape[0])
+    right = [(i, (i + 1) % peers) for i in range(peers)]
+    left = [(i, (i - 1) % peers) for i in range(peers)]
+    out = jnp.zeros((*features.shape[:0], peers * width, *features.shape[0 + 1 :]), features.dtype)
+    out = lax.dynamic_update_slice_in_dim(out, features, index * width, axis=0)
+    from_left = from_right = features
+    halfway = peers // 2
+    for turn in range(1, halfway + 1):
+        from_left = lax.ppermute(from_left, "ex", right)
+        out = lax.dynamic_update_slice_in_dim(
+            out, from_left, (index - turn) % peers * width, axis=0
+        )
+        if turn < peers - halfway:
+            from_right = lax.ppermute(from_right, "ex", left)
+            out = lax.dynamic_update_slice_in_dim(
+                out, from_right, (index + turn) % peers * width, axis=0
+            )
+    pool_rows = out
     targets = jnp.take(pool_rows, target_indices, axis=0)
     partial_dots = jnp.dot(features, targets.T, precision=lax.Precision.HIGHEST)
     scores = lax.psum(partial_dots, "param") / scale_k

time: 556 us -> 575 us (1.034)
  the two profiles are of different devices: /device:TPU:8 before, /device:TPU:32 now
where the time goes in v1:
time: 575 us; the launch traced here: 574 us
  waiting for transfers between devices  240 us (42%)
  blocking collectives  210 us (37%)
  matrix products  70.3 us (12%)
  starting transfers between devices  20.7 us (4%)
  between operations  16 us (3%)
  local copies, waits for them, and re-layouts  13.8 us (2%)
    reduce_scatter x1, waiting for transfers between devices, local(): lax.psum_scatter(partial_sums, 'param', scatter_dimension=1, tiled=True)  225 us
    psum x1, blocking collectives, local(): scores = lax.psum(partial_dots, 'param') / scale_k  138 us
    psum x1, blocking collectives, local(): total_sq = lax.psum(own_squares, 'param')  72.2 us
    dot_general x8, matrix products, accumulate(): jnp.dot(gradient_slab, signs, preferred_element_type=jnp.float32)  69.9 us
    ppermute x7, starting transfers between devices, local(): from_right = lax.ppermute(from_right, 'ex', left)  20.7 us
    ppermute x8, waiting for transfers between devices, local(): from_left = lax.ppermute(from_left, 'ex', right)  15.6 us
  transfers between devices with their start and end apart: 16, of which 9 were waited for; matrix products, arithmetic and copies ran while one was open for 0% of the time, Pallas kernels for 0%

profile of v1, /device:TPU:32, one launch (start us, length us, event | category | flops | bytes accessed | tf_op | source)
XLA Modules:
  0.0 574.2 jit_solution(8599972284594733491)
XLA Ops:
  7.2 1.4 fusion.24
  10.4 80.9 %while.12 = (s32[]{:T(128)}, f32[32,8192]{1,0:T(8,128)S(1)}, bf16[32,4096]{1,0:T(8,128)(2,1)}, s32[]{:T(128)}, s32[]{:T(128)}, /*index=5*/s32[]{:T(128)}, s32[4]...) while((s32[]{:T(128)}, f32[32,8192]{1,0:T(8,128)S(1)}, ...), condition=%wide.region_1.2_spmd.clone, body=%wide.region_0.1_spmd.clone.sunk | while | flops 323494912 | bytes 2200785 | solution.py:39
  10.5 1.3 slice.29
  11.8 8.7 %convolution_add_fusion.2 = f32[32,8192]{1,0:T(8,128)S(1)} fusion(s32[]{:T(128)} %get-tuple-element.189, s32[]{:T(128)} %bitcast.6, s32[8192]{0:T(1024)S(1)} %iota_multiply_fusion.2, s32[512]{0:T(512)S(1)} %add_multiply_fusion.2, f32[32,8192]{1,0:T(8,128)S(1)} %get-tuple-element.171, pred[]{:T(512)S(6)} %compare.18, ...), kind=kOutput, calls=%fused_computation.8.clone.1 | convolution fusion | flops 323485696 | bytes 2165765 | tf_op jit(solution)/shard_map/while/body/dot_general | solution.py:37
  20.6 1.3 slice.29
  21.9 8.7 %convolution_add_fusion.2 = f32[32,8192]{1,0:T(8,128)S(1)} fusion(s32[]{:T(128)} %get-tuple-element.189, s32[]{:T(128)} %bitcast.6, s32[8192]{0:T(1024)S(1)} %iota_multiply_fusion.2, s32[512]{0:T(512)S(1)} %add_multiply_fusion.2, f32[32,8192]{1,0:T(8,128)S(1)} %get-tuple-element.171, pred[]{:T(512)S(6)} %compare.18, ...), kind=kOutput, calls=%fused_computation.8.clone.1 | convolution fusion | flops 323485696 | bytes 2165765 | tf_op jit(solution)/shard_map/while/body/dot_general | solution.py:37
  32.0 8.7 %convolution_add_fusion.2 = f32[32,8192]{1,0:T(8,128)S(1)} fusion(s32[]{:T(128)} %get-tuple-element.189, s32[]{:T(128)} %bitcast.6, s32[8192]{0:T(1024)S(1)} %iota_multiply_fusion.2, s32[512]{0:T(512)S(1)} %add_multiply_fusion.2, f32[32,8192]{1,0:T(8,128)S(1)} %get-tuple-element.171, pred[]{:T(512)S(6)} %compare.18, ...), kind=kOutput, calls=%fused_computation.8.clone.1 | convolution fusion | flops 323485696 | bytes 2165765 | tf_op jit(solution)/shard_map/while/body/dot_general | solution.py:37
  42.1 8.7 %convolution_add_fusion.2 = f32[32,8192]{1,0:T(8,128)S(1)} fusion(s32[]{:T(128)} %get-tuple-element.189, s32[]{:T(128)} %bitcast.6, s32[8192]{0:T(1024)S(1)} %iota_multiply_fusion.2, s32[512]{0:T(512)S(1)} %add_multiply_fusion.2, f32[32,8192]{1,0:T(8,128)S(1)} %get-tuple-element.171, pred[]{:T(512)S(6)} %compare.18, ...), kind=kOutput, calls=%fused_computation.8.clone.1 | convolution fusion | flops 323485696 | bytes 2165765 | tf_op jit(solution)/shard_map/while/body/dot_general | solution.py:37
  52.2 8.7 %convolution_add_fusion.2 = f32[32,8192]{1,0:T(8,128)S(1)} fusion(s32[]{:T(128)} %get-tuple-element.189, s32[]{:T(128)} %bitcast.6, s32[8192]{0:T(1024)S(1)} %iota_multiply_fusion.2, s32[512]{0:T(512)S(1)} %add_multiply_fusion.2, f32[32,8192]{1,0:T(8,128)S(1)} %get-tuple-element.171, pred[]{:T(512)S(6)} %compare.18, ...), kind=kOutput, calls=%fused_computation.8.clone.1 | convolution fusion | flops 323485696 | bytes 2165765 | tf_op jit(solution)/shard_map/while/body/dot_general | solution.py:37
  61.0 1.3 slice.29
  62.3 8.7 %convolution_add_fusion.2 = f32[32,8192]{1,0:T(8,128)S(1)} fusion(s32[]{:T(128)} %get-tuple-element.189, s32[]{:T(128)} %bitcast.6, s32[8192]{0:T(1024)S(1)} %iota_multiply_fusion.2, s32[512]{0:T(512)S(1)} %add_multiply_fusion.2, f32[32,8192]{1,0:T(8,128)S(1)} %get-tuple-element.171, pred[]{:T(512)S(6)} %compare.18, ...), kind=kOutput, calls=%fused_computation.8.clone.1 | convolution fusion | flops 323485696 | bytes 2165765 | tf_op jit(solution)/shard_map/while/body/dot_general | solution.py:37
  72.5 8.7 %convolution_add_fusion.2 = f32[32,8192]{1,0:T(8,128)S(1)} fusion(s32[]{:T(128)} %get-tuple-element.189, s32[]{:T(128)} %bitcast.6, s32[8192]{0:T(1024)S(1)} %iota_multiply_fusion.2, s32[512]{0:T(512)S(1)} %add_multiply_fusion.2, f32[32,8192]{1,0:T(8,128)S(1)} %get-tuple-element.171, pred[]{:T(512)S(6)} %compare.18, ...), kind=kOutput, calls=%fused_computation.8.clone.1 | convolution fusion | flops 323485696 | bytes 2165765 | tf_op jit(solution)/shard_map/while/body/dot_general | solution.py:37
  81.3 1.3 slice.29
  82.6 8.7 %convolution_add_fusion.2 = f32[32,8192]{1,0:T(8,128)S(1)} fusion(s32[]{:T(128)} %get-tuple-element.189, s32[]{:T(128)} %bitcast.6, s32[8192]{0:T(1024)S(1)} %iota_multiply_fusion.2, s32[512]{0:T(512)S(1)} %add_multiply_fusion.2, f32[32,8192]{1,0:T(8,128)S(1)} %get-tuple-element.171, pred[]{:T(512)S(6)} %compare.18, ...), kind=kOutput, calls=%fused_computation.8.clone.1 | convolution fusion | flops 323485696 | bytes 2165765 | tf_op jit(solution)/shard_map/while/body/dot_general | solution.py:37
  92.4 224.8 %reduce-scatter.2.cloned.1.call-done = f32[32,256]{1,0:T(8,128)} async-done(((f32[32,8192]{1,0:T(8,128)}), f32[32,256]{1,0:T(8,128)}) %reduce-scatter.2.cloned.1.call-update) | async-done | bytes 32784 | tf_op jit(solution)/shard_map/reduce_scatter | solution.py:45
  318.1 72.2 %psum.14 = f32[32]{0:T(128)S(1)} all-reduce(f32[32]{0:T(128)S(1)} %multiply_reduce_fusion), channel_id=1, replica_groups=mesh['param'=32,'ex'=16] {'param'}, use_global_device_ids=true, to_apply=%region_4.5 | all-reduce | flops 32 | bytes 256 | tf_op jit(solution)/shard_map/psum | solution.py:47
  391.2 2.9 collective-permute-start.1
  394.2 1.6 collective-permute-done
  395.7 3.0 collective-permute-start.3
  398.7 1.6 collective-permute-done.2
  400.3 3.0 collective-permute-start.5
  403.3 1.6 collective-permute-done.4
  404.9 3.0 collective-permute-start.7
  407.8 1.6 collective-permute-done.6
  409.4 3.0 collective-permute-start.9
  412.4 1.6 collective-permute-done.8
  414.0 3.0 collective-permute-start.11
  416.9 1.6 collective-permute-done.10
  418.5 3.0 collective-permute-start.13
  421.5 1.6 collective-permute-done.12
  423.1 4.5 collective-permute-done.14
  429.0 137.7 %psum.15 = f32[32,256]{1,0:T(8,128)S(1)} all-reduce(f32[32,256]{1,0:T(8,128)S(1)} %fusion.19), channel_id=1, replica_groups=mesh['param'=32,'ex'=16] {'param'}, use_global_device_ids=true, to_apply=%region_5.6 | all-reduce | flops 8192 | bytes 65536 | tf_op jit(solution)/shard_map/psum | solution.py:69
  (69 shorter events, 10.3 us)
Async XLA Ops:
  7.2 310.0 %reduce-scatter.2.cloned.1.call-start = ((), (), s32[]{:S(2)}) async-start(), calls=%async_computation.1 | async-start | bytes 1081344 | tf_op jit(solution)/shard_map/reduce_scatter | solution.py:45
  91.3 1.0 copy-start
  91.3 1.0 copy-start.2
  391.2 37.4 %copy-start.1 = (f32[32,256]{1,0:T(8,128)}, f32[32,256]{1,0:T(8,128)S(1)}, u32[]{:S(2)}) copy-start(f32[32,256]{1,0:T(8,128)S(1)} %get-tuple-element.105) | copy-start | bytes 98308
  391.2 4.6 collective-permute-start
  391.2 4.5 collective-permute-start.1
  395.7 4.6 collective-permute-start.2
  395.7 4.6 collective-permute-start.3
  400.3 4.6 collective-permute-start.4
  400.3 4.6 collective-permute-start.5
  404.8 4.6 collective-permute-start.6
  404.9 4.6 collective-permute-start.7
  409.4 4.6 collective-permute-start.8
  409.4 4.6 collective-permute-start.9
  413.9 4.6 collective-permute-start.10
  414.0 4.6 collective-permute-start.11
  418.5 4.6 collective-permute-start.12
  418.5 4.6 collective-permute-start.13
  423.0 4.6 collective-permute-start.14
Sparse Core Ops, SparseCore 0:
  92.4 224.7 reduce-scatter.1
